TPU v7x, 256 devices: a whole 4x4x8 slice. The times are simulated.
256 devices in a mesh: det: 16 (over z, core), orb: 16 (over x, y).
Axes of the slice: x: 4, y: 4, z: 8, core: 2. Of those that a mesh axis runs over, the one named last changes fastest.
Arguments:
- orbitals: bfloat16 [64, 1024, 256], P('det', 'orb'), may hold values from -0.06 to 1.06
- dfit: bfloat16 [64, 1024, 1024], P('orb'), may hold values from -0.5 to 0.5, as said below
- pair_left: int32 [32], P('det'), may hold values from 0 to 63, as said below
- pair_right: int32 [32], P('det'), may hold values from 0 to 63
- pair_count: int32 [16], P('det'), may hold values from 1 to 2, as said below
- pair_weight: float32 [32], P('det'), may hold values from 1 to 4
- aux_screen: int32 [32, 64], P('det', 'orb'), may hold values 0 or 1
Outputs:
- gradient: float32 [64, 1024, 256], P('det', 'orb')
Inputs may be any that keep to these rules, and one draw needn't show every extreme that they name: `pair_left`: slot s names a determinant among numbers (s // 2) * 4 to (s // 2 + 1) * 4 - 1. `pair_count`: some det index has all 2 slots live. `dfit`: every matrix is symmetric.
All inputs are finite; a program needn't handle non-finite values. No bound on the sum of `aux_screen` on one device may be relied on, other than what follows from the above.
Results may differ from a plain program's by a relative error of at most 0.0022.
Values may be sent and summed in bfloat16 or wider, within the bound.
No kernel may reach another device: no remote copies, remote signals or barrier semaphores. Data moves between devices by JAX's collectives and lax.ppermute only.
A program may use at most 64 MiB of HBM per device.

v0:
```python
import jax
import jax.numpy as jnp
from jax import lax
from jax.sharding import PartitionSpec as P

NS = 3


def newton(correlation):
    eye = jnp.eye(correlation.shape[-1], dtype=jnp.float32)
    inverse = jnp.broadcast_to(eye, correlation.shape)
    for sweep in range(NS):
        product = jnp.einsum("bij,bjk->bik", correlation, inverse, precision=lax.Precision.HIGHEST)
        inverse = jnp.einsum(
            "bij,bjk->bik", inverse, 2.0 * eye - product, precision=lax.Precision.HIGHEST
        )
    return inverse


def process(dfit, left_rows, right_rows, weights, screen):
    correlation_part = jnp.einsum(
        "brc,brd->bcd", left_rows, right_rows, preferred_element_type=jnp.float32
    )
    correlation = lax.psum(correlation_part, "orb")
    inverse = newton(correlation)
    moved_rows = jnp.einsum(
        "brc,bcd->brd", right_rows.astype(jnp.float32), inverse, precision=lax.Precision.HIGHEST
    ).astype(jnp.bfloat16)
    left_full, moved_full = (
        lax.all_gather(left_rows, "orb", axis=1, tiled=True),
        lax.all_gather(moved_rows, "orb", axis=1, tiled=True),
    )
    applied = jnp.einsum(
        "qst,btc->bqsc", dfit, moved_full, preferred_element_type=jnp.float32
    ).astype(jnp.bfloat16)
    projected = jnp.einsum(
        "bsc,qst->bqct", left_full, dfit, preferred_element_type=jnp.float32
    ).astype(jnp.bfloat16)
    exchange = jnp.einsum(
        "bqct,btd->bqcd", projected, moved_full, preferred_element_type=jnp.float32
    )
    factor = 2.0 * weights[:, None, None, None] * screen.astype(jnp.float32)[:, :, None, None]
    scaled = (factor * exchange).astype(jnp.bfloat16)
    left_term = jnp.einsum("bqsc,bqdc->sbd", applied, scaled, preferred_element_type=jnp.float32)
    moved_term = jnp.einsum("bqcs,bqcd->sbd", projected, scaled, preferred_element_type=jnp.float32)
    summed = lax.psum_scatter(
        jnp.concatenate([left_term, moved_term], axis=1), "orb", scatter_dimension=0, tiled=True
    )
    batch = left_rows.shape[0]
    left_grad = jnp.transpose(summed[:, :batch], (1, 0, 2))
    moved_grad = jnp.transpose(summed[:, batch:], (1, 0, 2))
    right_grad = jnp.einsum("brc,bdc->brd", moved_grad, inverse, precision=lax.Precision.HIGHEST)
    return (left_grad, right_grad)


def local(orbitals, dfit, pair_left, pair_right, pair_count, pair_weight, aux_screen):
    det_local = orbitals.shape[0]
    capacity = pair_left.shape[0]
    slot_index = jnp.arange(capacity, dtype=jnp.int32)
    weights = jnp.where(slot_index < pair_count[0], pair_weight, jnp.zeros_like(pair_weight))
    left_local = pair_left % det_local
    left_rows = jnp.take(orbitals, left_local, axis=0)
    everyone = lax.all_gather(orbitals, "det", axis=0, tiled=True)
    right_rows = jnp.take(everyone, pair_right, axis=0)

    def one_slot(slot, grads):

        def select_slot(array):
            return lax.dynamic_slice_in_dim(array, slot, 1, 0)

        left_one, right_one = process(
            dfit,
            select_slot(left_rows),
            select_slot(right_rows),
            select_slot(weights),
            select_slot(aux_screen),
        )
        return (
            lax.dynamic_update_slice_in_dim(grads[0], left_one, slot, 0),
            lax.dynamic_update_slice_in_dim(grads[1], right_one, slot, 0),
        )

    zeros = jnp.zeros(left_rows.shape, jnp.float32)
    left_grad, right_grad = lax.fori_loop(0, capacity, one_slot, (zeros, zeros))
    owners = (left_local[:, None] == jnp.arange(det_local, dtype=jnp.int32)[None, :]).astype(
        jnp.float32
    )
    own_sum = jnp.einsum("pn,prc->nrc", owners, left_grad, precision=lax.Precision.HIGHEST)
    places = jnp.arange(det_local * lax.axis_size("det"), dtype=jnp.int32)
    match = (pair_right[:, None] == places[None, :]).astype(jnp.float32)
    returned = lax.psum_scatter(
        jnp.einsum("pn,prc->nrc", match, right_grad, precision=lax.Precision.HIGHEST),
        "det",
        scatter_dimension=0,
        tiled=True,
    )
    return own_sum + returned


def solution(mesh):
    in_specs = (
        P("det", "orb", None),
        P("orb", None, None),
        P("det"),
        P("det"),
        P("det"),
        P("det"),
        P("det", "orb"),
    )
    out_specs = P("det", "orb", None)
    return jax.shard_map(local, mesh=mesh, in_specs=in_specs, out_specs=out_specs, check_vma=False)
```

profile of v0, /device:TPU:4, one launch (start us, length us, event | category | flops | bytes accessed | tf_op | source)
XLA Modules:
  0.0 620.7 jit_solution(5396601231880543745)
XLA Ops:
  8.6 1.5 gather_fusion
  12.1 39.4 %all-gather.5.cloned.1.call-done = bf16[64,64,256]{2,1,0:T(8,128)(2,1)} async-done(((bf16[4,64,256]{2,1,0:T(8,128)(2,1)}), bf16[64,64,256]{2,1,0:T(8,128)(2,1)}) %all-gather.5.cloned.1.call-update) | async-done | bytes 2097168 | tf_op jit(solution)/shard_map/all_gather | solution.py:63
  51.6 2.1 gather_fusion.1
  53.8 486.6 %while.15 = (s32[]{:T(128)}, f32[2,64,256]{2,0,1:T(2,128)}, f32[2,64,256]{2,0,1:T(2,128)}, f32[2]{0:T(128)S(1)}, s32[2,4]{1,0:T(2,128)}, /*index=5*/bf16[2,64,25...) while((s32[]{:T(128)}, f32[2,64,256]{2,0,1:T(2,128)}, ...), condition=%wide.region_3.4_spmd, body=%wide.region_0.3_spmd.sunk | while | flops 7227064320 | bytes 65279744 | solution.py:84
  54.9 23.7 %all_gather.19 = bf16[1,1024,256]{2,1,0:T(8,128)(2,1)S(1)} all-gather(bf16[1,64,256]{2,1,0:T(8,128)(2,1)S(1)} %constant_dynamic-slice_fusion.6), channel_id=1, replica_groups=mesh['det'=16,'orb'=16] {'orb'}, dimensions={1}, use_global_device_ids=true | all-gather | bytes 557056 | tf_op jit(solution)/shard_map/while/body/eval_jaxpr/all_gather | solution.py:30
  78.5 5.8 convolution_convert_fusion.4
  85.6 64.8 %all-reduce.6.cloned.1.call-done = f32[256,256]{1,0:T(8,128)} async-done(((f32[256,256]{1,0:T(8,128)}), f32[256,256]{1,0:T(8,128)}) %all-reduce.6.cloned.1.call-update) | async-done | bytes 262160 | tf_op jit(solution)/shard_map/while/body/eval_jaxpr/psum | solution.py:24
  154.7 22.7 %all-gather.2 = bf16[1024,256]{1,0:T(8,128)(2,1)S(1)} all-gather(bf16[64,256]{1,0:T(8,128)(2,1)S(1)} %convolution_convert_fusion.5), channel_id=2, replica_groups=mesh['det'=16,'orb'=16] {'orb'}, dimensions={0}, use_global_device_ids=true | all-gather | bytes 557056 | tf_op jit(solution)/shard_map/while/body/eval_jaxpr/all_gather | solution.py:31
  180.5 7.7 %fusion.137 = f32[1024,1,256]{0,2,1:T(8,128)} fusion(bf16[4,256,256]{2,1,0:T(8,128)(2,1)} %copy-done.1, bf16[4,1024,1024]{2,1,0:T(8,128)(2,1)} %get-tuple-element.280, bf16[1024,256]{1,0:T(8,128)(2,1)} %copy-done.2), kind=kOutput, calls=%fused_computation.12.clone.1 | convolution fusion | flops 2685403136 | bytes 10485760 | tf_op jit(solution)/shard_map/while/body/eval_jaxpr/bqsc,bqdc->sbd/dot_general | solution.py:44
  188.2 1.4 pad_maximum_fusion.2
  189.6 2.4 copy.46
  193.8 98.1 %all-reduce.8.cloned.1.call-done = f32[1024,2,256]{2,1,0:T(2,128)} async-done(((f32[1024,2,256]{2,1,0:T(2,128)}), f32[1024,2,256]{2,1,0:T(2,128)}) %all-reduce.8.cloned.1.call-update) | async-done | bytes 2097168 | tf_op jit(solution)/shard_map/while
  297.0 23.4 %all_gather.19 = bf16[1,1024,256]{2,1,0:T(8,128)(2,1)S(1)} all-gather(bf16[1,64,256]{2,1,0:T(8,128)(2,1)S(1)} %constant_dynamic-slice_fusion.6), channel_id=1, replica_groups=mesh['det'=16,'orb'=16] {'orb'}, dimensions={1}, use_global_device_ids=true | all-gather | bytes 557056 | tf_op jit(solution)/shard_map/while/body/eval_jaxpr/all_gather | solution.py:30
  320.4 5.8 convolution_convert_fusion.4
  327.4 67.3 %all-reduce.6.cloned.1.call-done = f32[256,256]{1,0:T(8,128)} async-done(((f32[256,256]{1,0:T(8,128)}), f32[256,256]{1,0:T(8,128)}) %all-reduce.6.cloned.1.call-update) | async-done | bytes 262160 | tf_op jit(solution)/shard_map/while/body/eval_jaxpr/psum | solution.py:24
  399.1 22.7 %all-gather.2 = bf16[1024,256]{1,0:T(8,128)(2,1)S(1)} all-gather(bf16[64,256]{1,0:T(8,128)(2,1)S(1)} %convolution_convert_fusion.5), channel_id=2, replica_groups=mesh['det'=16,'orb'=16] {'orb'}, dimensions={0}, use_global_device_ids=true | all-gather | bytes 557056 | tf_op jit(solution)/shard_map/while/body/eval_jaxpr/all_gather | solution.py:31
  424.9 7.7 %fusion.137 = f32[1024,1,256]{0,2,1:T(8,128)} fusion(bf16[4,256,256]{2,1,0:T(8,128)(2,1)} %copy-done.1, bf16[4,1024,1024]{2,1,0:T(8,128)(2,1)} %get-tuple-element.280, bf16[1024,256]{1,0:T(8,128)(2,1)} %copy-done.2), kind=kOutput, calls=%fused_computation.12.clone.1 | convolution fusion | flops 2685403136 | bytes 10485760 | tf_op jit(solution)/shard_map/while/body/eval_jaxpr/bqsc,bqdc->sbd/dot_general | solution.py:44
  432.5 1.4 pad_maximum_fusion.2
  433.9 2.4 copy.46
  438.2 98.1 %all-reduce.8.cloned.1.call-done = f32[1024,2,256]{2,1,0:T(2,128)} async-done(((f32[1024,2,256]{2,1,0:T(2,128)}), f32[1024,2,256]{2,1,0:T(2,128)}) %all-reduce.8.cloned.1.call-update) | async-done | bytes 2097168 | tf_op jit(solution)/shard_map/while
  540.4 2.8 fusion.39
  543.2 4.4 copy.30
  549.0 63.2 %reduce-scatter.2.cloned.1.call-done = f32[4,64,256]{2,1,0:T(8,128)} async-done(((f32[64,64,256]{2,1,0:T(8,128)}), f32[4,64,256]{2,1,0:T(8,128)}) %reduce-scatter.2.cloned.1.call-update) | async-done | bytes 262160 | tf_op jit(solution)/shard_map/reduce_scatter | solution.py:91
  612.2 1.7 copy_add_fusion
  (102 shorter events, 33.4 us)
Async XLA Ops:
  6.5 45.0 %all-gather.5.cloned.1.call-start = ((), (), s32[]{:S(2)}) async-start(), calls=%async_computation.1 | async-start | bytes 2228224 | tf_op jit(solution)/shard_map/all_gather | solution.py:63
  53.8 486.6 %copy-start.9 = (s32[2]{0:T(128)S(1)}, s32[2]{0:T(128)}, u32[]{:S(2)}) copy-start(s32[2]{0:T(128)} %param.12) | copy-start | bytes 28
  53.8 96.5 %all-reduce.6.cloned.1.call-start = ((), (), s32[]{:S(2)}) async-start(), calls=%async_computation.3 | async-start | bytes 524288 | tf_op jit(solution)/shard_map/while/body/eval_jaxpr/psum | solution.py:24
  54.8 237.1 %all-reduce.8.cloned.1.call-start = ((), (), s32[]{:S(2)}) async-start(), calls=%async_computation.4 | async-start | bytes 4194304 | tf_op jit(solution)/shard_map/while
  78.5 7.0 %copy-start.8 = (s32[2,4]{1,0:T(2,128)S(1)}, s32[2,4]{1,0:T(2,128)}, u32[]{:S(2)}) copy-start(s32[2,4]{1,0:T(2,128)} %get-tuple-element.278) | copy-start | bytes 100 | tf_op jit(solution)/shard_map/while
  150.4 3.3 copy-start
  177.4 0.8 copy-start.2
  179.0 0.8 copy-start.1
  191.9 0.7 copy-start.10
  192.0 101.5 %copy-start.5 = (f32[2,64,256]{2,0,1:T(2,128)S(1)}, f32[2,64,256]{2,0,1:T(2,128)}, u32[]{:S(2)}) copy-start(f32[2,64,256]{2,0,1:T(2,128)} %get-tuple-element.260) | copy-start | bytes 393220 | tf_op jit(solution)/shard_map/while
  192.0 102.5 %copy-start.3 = (f32[2,64,256]{2,0,1:T(2,128)S(1)}, f32[2,64,256]{2,0,1:T(2,128)}, u32[]{:S(2)}) copy-start(f32[2,64,256]{2,0,1:T(2,128)} %get-tuple-element.261) | copy-start | bytes 393220 | tf_op jit(solution)/shard_map/while
  294.4 1.0 copy-start.6
  296.0 98.7 %all-reduce.6.cloned.1.call-start = ((), (), s32[]{:S(2)}) async-start(), calls=%async_computation.3 | async-start | bytes 524288 | tf_op jit(solution)/shard_map/while/body/eval_jaxpr/psum | solution.py:24
  296.9 239.4 %all-reduce.8.cloned.1.call-start = ((), (), s32[]{:S(2)}) async-start(), calls=%async_computation.4 | async-start | bytes 4194304 | tf_op jit(solution)/shard_map/while
  320.4 7.0 %copy-start.8 = (s32[2,4]{1,0:T(2,128)S(1)}, s32[2,4]{1,0:T(2,128)}, u32[]{:S(2)}) copy-start(s32[2,4]{1,0:T(2,128)} %get-tuple-element.278) | copy-start | bytes 100 | tf_op jit(solution)/shard_map/while
  394.7 3.3 copy-start
  421.8 0.8 copy-start.2
  423.3 0.8 copy-start.1
  436.3 0.7 copy-start.10
  436.3 101.5 %copy-start.5 = (f32[2,64,256]{2,0,1:T(2,128)S(1)}, f32[2,64,256]{2,0,1:T(2,128)}, u32[]{:S(2)}) copy-start(f32[2,64,256]{2,0,1:T(2,128)} %get-tuple-element.260) | copy-start | bytes 393220 | tf_op jit(solution)/shard_map/while
  436.3 102.5 %copy-start.3 = (f32[2,64,256]{2,0,1:T(2,128)S(1)}, f32[2,64,256]{2,0,1:T(2,128)}, u32[]{:S(2)}) copy-start(f32[2,64,256]{2,0,1:T(2,128)} %get-tuple-element.261) | copy-start | bytes 393220 | tf_op jit(solution)/shard_map/while
  538.8 1.0 copy-start.6
  540.4 71.8 %reduce-scatter.2.cloned.1.call-start = ((), (), s32[]{:S(2)}) async-start(), calls=%async_computation.2 | async-start | bytes 4456448 | tf_op jit(solution)/shard_map/reduce_scatter | solution.py:91
  547.6 0.9 copy-start.7
  (2 other events, 1.3 us)
Sparse Core Ops, SparseCore 0:
  9.2 42.3 all-gather.4
  57.8 92.5 all-reduce.5
  192.1 99.8 all-reduce.7
  299.7 94.9 all-reduce.5
  436.4 99.8 all-reduce.7
  547.7 64.3 reduce-scatter.1
where the time goes:
time: 621 us
  waiting for transfers between devices  432 us (70%)
  blocking collectives  92.5 us (15%)
  matrix products  44.2 us (7%)
  local copies, waits for them, and re-layouts  27.8 us (4%)
  between operations  14.1 us (2%)
  other arithmetic  7.37 us (1%)
    while x6, waiting for transfers between devices  196 us
    psum x2, waiting for transfers between devices, process(): correlation = lax.psum(correlation_part, 'orb')  132 us
    reduce_scatter x1, waiting for transfers between devices, local(): lax.psum_scatter(jnp.einsum('pn,prc->nrc', match, right_grad, precision=l...  63.2 us
    all_gather x2, blocking collectives, process(): lax.all_gather(left_rows, 'orb', axis=1, tiled=True)  47 us
    all_gather x2, blocking collectives, process(): lax.all_gather(moved_rows, 'orb', axis=1, tiled=True)  45.4 us
    all_gather x1, waiting for transfers between devices, local(): everyone = lax.all_gather(orbitals, 'det', axis=0, tiled=True)  39.4 us
    dot_general x2, matrix products, process(): jnp.einsum('bqsc,bqdc->sbd', applied, scaled, preferred_element_type=jnp....  15.3 us
  transfers between devices with their start and end apart: 6, of which 6 were waited for; matrix products, arithmetic and copies ran while one was open for 3% of the time, Pallas kernels for 0%

commit v1 on v0

--- a/solution.py
+++ b/solution.py
@@ -1,9 +1,19 @@
+import functools
 import jax
 import jax.numpy as jnp
 from jax import lax
 from jax.sharding import PartitionSpec as P
+from jax.lax import all_gather
 
 NS = 3
+
+
+def work_lane(target, link_axis):
+    small = all_gather(target, link_axis).sum(axis=0)
+    return small
+
+
+form_the_space = functools.partial(work_lane, link_axis="orb")
 
 
 def newton(correlation):
@@ -21,7 +31,7 @@
     correlation_part = jnp.einsum(
         "brc,brd->bcd", left_rows, right_rows, preferred_element_type=jnp.float32
     )
-    correlation = lax.psum(correlation_part, "orb")
+    correlation = form_the_space(correlation_part)
     inverse = newton(correlation)
     moved_rows = jnp.einsum(
         "brc,bcd->brd", right_rows.astype(jnp.float32), inverse, precision=lax.Precision.HIGHEST

time: 621 us -> 546 us (0.88)
  waiting for transfers between devices: 432 us -> 354 us
  other arithmetic: 7.37 us -> 13.7 us
    psum x2 -> x0, waiting for transfers between devices: 132 us -> none  [process(): correlation = lax.psum(correlation_part, 'orb')]
    all_gather x0 -> x2, waiting for transfers between devices: none -> 54 us  [work_lane(): small = all_gather(target, link_axis).sum(axis=0)]
  transfers between devices with their start and end apart: 6 -> 6, of which waited for: 6 -> 6; matrix products, arithmetic and copies ran while one was open for 3% -> 4% of each run, Pallas kernels for 0% -> 0%
where the time goes in v1:
time: 546 us; the launch traced here: 545 us
  waiting for transfers between devices  354 us (65%)
  blocking collectives  92.4 us (17%)
  matrix products  40.2 us (7%)
  local copies, waits for them, and re-layouts  27.7 us (5%)
  between operations  14.1 us (3%)
  other arithmetic  13.7 us (3%)
    while x6, waiting for transfers between devices  197 us
    reduce_scatter x1, waiting for transfers between devices, local(): lax.psum_scatter(jnp.einsum('pn,prc->nrc', match, right_grad, precision=l...  63.2 us
    all_gather x2, waiting for transfers between devices, work_lane(): small = all_gather(target, link_axis).sum(axis=0)  54 us
    all_gather x2, blocking collectives, process(): lax.all_gather(left_rows, 'orb', axis=1, tiled=True)  48.1 us
    all_gather x2, blocking collectives, process(): lax.all_gather(moved_rows, 'orb', axis=1, tiled=True)  44.3 us
    all_gather x1, waiting for transfers between devices, local(): everyone = lax.all_gather(orbitals, 'det', axis=0, tiled=True)  39.4 us
    dot_general x2, matrix products, process(): jnp.einsum('bqsc,bqdc->sbd', applied, scaled, preferred_element_type=jnp....  15.3 us
    dot_general x2, matrix products, process(): jnp.einsum('bsc,qst->bqct', left_full, dfit, preferred_element_type=jnp.f...  11.5 us
  transfers between devices with their start and end apart: 6, of which 6 were waited for; matrix products, arithmetic and copies ran while one was open for 4% of the time, Pallas kernels for 0%

profile of v1, /device:TPU:4, one launch (start us, length us, event | category | flops | bytes accessed | tf_op | source)
XLA Modules:
  0.0 545.2 jit_solution(15788098546302673662)
XLA Ops:
  8.6 1.5 gather_fusion
  12.1 39.4 %all-gather.9.cloned.1.call-done = bf16[64,64,256]{2,1,0:T(8,128)(2,1)} async-done(((bf16[4,64,256]{2,1,0:T(8,128)(2,1)}), bf16[64,64,256]{2,1,0:T(8,128)(2,1)}) %all-gather.9.cloned.1.call-update) | async-done | bytes 2097168 | tf_op jit(solution)/shard_map/all_gather | solution.py:73
  51.6 2.1 gather_fusion.1
  53.8 411.1 %while.15 = (s32[]{:T(128)}, f32[2,64,256]{2,0,1:T(2,128)}, f32[2,64,256]{2,0,1:T(2,128)}, f32[2]{0:T(128)S(1)}, s32[2,4]{1,0:T(2,128)}, /*index=5*/bf16[2,64,25...) while((s32[]{:T(128)}, f32[2,64,256]{2,0,1:T(2,128)}, ...), condition=%wide.region_3.4_spmd, body=%wide.region_0.3_spmd.sunk | while | flops 7227981824 | bytes 80483936 | solution.py:94
  56.7 24.2 %all_gather.33 = bf16[1,1024,256]{2,1,0:T(8,128)(2,1)S(1)} all-gather(bf16[1,64,256]{2,1,0:T(8,128)(2,1)S(1)} %constant_dynamic-slice_fusion.6), channel_id=1, replica_groups=mesh['det'=16,'orb'=16] {'orb'}, dimensions={1}, use_global_device_ids=true | all-gather | bytes 557056 | tf_op jit(solution)/shard_map/while/body/eval_jaxpr/all_gather | solution.py:40
  80.9 5.8 %convolution_convert_fusion.4 = bf16[256,4,1024]{2,0,1:T(8,128)(2,1)S(1)} fusion(bf16[4,1024,1024]{2,1,0:T(8,128)(2,1)} %get-tuple-element.282, bf16[1,1024,256]{2,1,0:T(8,128)(2,1)S(1)} %all_gather.33), kind=kOutput, calls=%fused_computation.10.clone.1 | convolution fusion | flops 2148532224 | bytes 11010048 | tf_op jit(solution)/shard_map/while/body/eval_jaxpr/bsc,qst->bqct/dot_general | solution.py:46
  86.7 25.9 %all-gather.11.cloned.1.call-done = f32[4096,256]{1,0:T(8,128)} async-done(((f32[256,256]{1,0:T(8,128)}), f32[4096,256]{1,0:T(8,128)}) %all-gather.11.cloned.1.call-update) | async-done | bytes 4194320 | tf_op jit(solution)/shard_map/while/body/eval_jaxpr/all_gather | solution.py:12
  112.6 2.5 reduce.5
  117.4 22.2 %all-gather.5 = bf16[1024,256]{1,0:T(8,128)(2,1)S(1)} all-gather(bf16[64,256]{1,0:T(8,128)(2,1)S(1)} %convolution_convert_fusion.5), channel_id=3, replica_groups=mesh['det'=16,'orb'=16] {'orb'}, dimensions={0}, use_global_device_ids=true | all-gather | bytes 557056 | tf_op jit(solution)/shard_map/while/body/eval_jaxpr/all_gather | solution.py:41
  142.7 7.6 %fusion.137 = f32[1024,1,256]{0,2,1:T(8,128)} fusion(bf16[4,256,256]{2,1,0:T(8,128)(2,1)} %copy-done, bf16[4,1024,1024]{2,1,0:T(8,128)(2,1)} %get-tuple-element.282, bf16[1024,256]{1,0:T(8,128)(2,1)} %copy-done.1), kind=kOutput, calls=%fused_computation.12.clone.1 | convolution fusion | flops 2685403136 | bytes 10485760 | tf_op jit(solution)/shard_map/while/body/eval_jaxpr/bqsc,bqdc->sbd/dot_general | solution.py:54
  151.7 2.4 copy.46
  155.9 98.4 %all-reduce.5.cloned.1.call-done = f32[1024,2,256]{2,1,0:T(2,128)} async-done(((f32[1024,2,256]{2,1,0:T(2,128)}), f32[1024,2,256]{2,1,0:T(2,128)}) %all-reduce.5.cloned.1.call-update) | async-done | bytes 2097168 | tf_op jit(solution)/shard_map/while
  261.3 23.9 %all_gather.33 = bf16[1,1024,256]{2,1,0:T(8,128)(2,1)S(1)} all-gather(bf16[1,64,256]{2,1,0:T(8,128)(2,1)S(1)} %constant_dynamic-slice_fusion.6), channel_id=1, replica_groups=mesh['det'=16,'orb'=16] {'orb'}, dimensions={1}, use_global_device_ids=true | all-gather | bytes 557056 | tf_op jit(solution)/shard_map/while/body/eval_jaxpr/all_gather | solution.py:40
  285.2 5.8 %convolution_convert_fusion.4 = bf16[256,4,1024]{2,0,1:T(8,128)(2,1)S(1)} fusion(bf16[4,1024,1024]{2,1,0:T(8,128)(2,1)} %get-tuple-element.282, bf16[1,1024,256]{2,1,0:T(8,128)(2,1)S(1)} %all_gather.33), kind=kOutput, calls=%fused_computation.10.clone.1 | convolution fusion | flops 2148532224 | bytes 11010048 | tf_op jit(solution)/shard_map/while/body/eval_jaxpr/bsc,qst->bqct/dot_general | solution.py:46
  290.9 28.1 %all-gather.11.cloned.1.call-done = f32[4096,256]{1,0:T(8,128)} async-done(((f32[256,256]{1,0:T(8,128)}), f32[4096,256]{1,0:T(8,128)}) %all-gather.11.cloned.1.call-update) | async-done | bytes 4194320 | tf_op jit(solution)/shard_map/while/body/eval_jaxpr/all_gather | solution.py:12
  319.0 2.5 reduce.5
  323.9 22.2 %all-gather.5 = bf16[1024,256]{1,0:T(8,128)(2,1)S(1)} all-gather(bf16[64,256]{1,0:T(8,128)(2,1)S(1)} %convolution_convert_fusion.5), channel_id=3, replica_groups=mesh['det'=16,'orb'=16] {'orb'}, dimensions={0}, use_global_device_ids=true | all-gather | bytes 557056 | tf_op jit(solution)/shard_map/while/body/eval_jaxpr/all_gather | solution.py:41
  349.1 7.6 %fusion.137 = f32[1024,1,256]{0,2,1:T(8,128)} fusion(bf16[4,256,256]{2,1,0:T(8,128)(2,1)} %copy-done, bf16[4,1024,1024]{2,1,0:T(8,128)(2,1)} %get-tuple-element.282, bf16[1024,256]{1,0:T(8,128)(2,1)} %copy-done.1), kind=kOutput, calls=%fused_computation.12.clone.1 | convolution fusion | flops 2685403136 | bytes 10485760 | tf_op jit(solution)/shard_map/while/body/eval_jaxpr/bqsc,bqdc->sbd/dot_general | solution.py:54
  358.2 2.4 copy.46
  362.4 98.4 %all-reduce.5.cloned.1.call-done = f32[1024,2,256]{2,1,0:T(2,128)} async-done(((f32[1024,2,256]{2,1,0:T(2,128)}), f32[1024,2,256]{2,1,0:T(2,128)}) %all-reduce.5.cloned.1.call-update) | async-done | bytes 2097168 | tf_op jit(solution)/shard_map/while
  464.9 2.8 fusion.39
  467.7 4.4 copy.30
  473.5 63.2 %reduce-scatter.2.cloned.1.call-done = f32[4,64,256]{2,1,0:T(8,128)} async-done(((f32[64,64,256]{2,1,0:T(8,128)}), f32[4,64,256]{2,1,0:T(8,128)}) %reduce-scatter.2.cloned.1.call-update) | async-done | bytes 262160 | tf_op jit(solution)/shard_map/reduce_scatter | solution.py:101
  536.7 1.7 copy_add_fusion
  (96 shorter events, 33.6 us)
Async XLA Ops:
  6.5 45.0 %all-gather.9.cloned.1.call-start = ((), (), s32[]{:S(2)}) async-start(), calls=%async_computation.1 | async-start | bytes 2228224 | tf_op jit(solution)/shard_map/all_gather | solution.py:73
  53.8 411.1 %copy-start.7 = (s32[2]{0:T(128)S(1)}, s32[2]{0:T(128)}, u32[]{:S(2)}) copy-start(s32[2]{0:T(128)} %param.12) | copy-start | bytes 28
  53.8 58.8 %all-gather.11.cloned.1.call-start = ((), (), s32[]{:S(2)}) async-start(), calls=%async_computation.3 | async-start | bytes 4456448 | tf_op jit(solution)/shard_map/while/body/eval_jaxpr/all_gather | solution.py:12
  54.8 199.6 %all-reduce.5.cloned.1.call-start = ((), (), s32[]{:S(2)}) async-start(), calls=%async_computation.4 | async-start | bytes 4194304 | tf_op jit(solution)/shard_map/while
  139.6 0.8 copy-start.1
  141.1 0.8 copy-start
  154.1 0.7 copy-start.8
  154.1 101.8 %copy-start.4 = (f32[2,64,256]{2,0,1:T(2,128)S(1)}, f32[2,64,256]{2,0,1:T(2,128)}, u32[]{:S(2)}) copy-start(f32[2,64,256]{2,0,1:T(2,128)} %get-tuple-element.261) | copy-start | bytes 393220 | tf_op jit(solution)/shard_map/while
  154.1 102.7 %copy-start.2 = (f32[2,64,256]{2,0,1:T(2,128)S(1)}, f32[2,64,256]{2,0,1:T(2,128)}, u32[]{:S(2)}) copy-start(f32[2,64,256]{2,0,1:T(2,128)} %get-tuple-element.262) | copy-start | bytes 393220 | tf_op jit(solution)/shard_map/while
  256.8 1.0 copy-start.5
  257.8 0.7 copy-start.3
  258.4 60.6 %all-gather.11.cloned.1.call-start = ((), (), s32[]{:S(2)}) async-start(), calls=%async_computation.3 | async-start | bytes 4456448 | tf_op jit(solution)/shard_map/while/body/eval_jaxpr/all_gather | solution.py:12
  259.4 201.5 %all-reduce.5.cloned.1.call-start = ((), (), s32[]{:S(2)}) async-start(), calls=%async_computation.4 | async-start | bytes 4194304 | tf_op jit(solution)/shard_map/while
  346.0 0.8 copy-start.1
  347.6 0.8 copy-start
  360.6 0.7 copy-start.8
  360.6 101.8 %copy-start.4 = (f32[2,64,256]{2,0,1:T(2,128)S(1)}, f32[2,64,256]{2,0,1:T(2,128)}, u32[]{:S(2)}) copy-start(f32[2,64,256]{2,0,1:T(2,128)} %get-tuple-element.261) | copy-start | bytes 393220 | tf_op jit(solution)/shard_map/while
  360.6 102.7 %copy-start.2 = (f32[2,64,256]{2,0,1:T(2,128)S(1)}, f32[2,64,256]{2,0,1:T(2,128)}, u32[]{:S(2)}) copy-start(f32[2,64,256]{2,0,1:T(2,128)} %get-tuple-element.262) | copy-start | bytes 393220 | tf_op jit(solution)/shard_map/while
  463.3 1.0 copy-start.5
  464.2 0.7 copy-start.3
  464.9 71.8 %reduce-scatter.2.cloned.1.call-start = ((), (), s32[]{:S(2)}) async-start(), calls=%async_computation.2 | async-start | bytes 4456448 | tf_op jit(solution)/shard_map/reduce_scatter | solution.py:101
  472.1 0.9 copy-start.6
Sparse Core Ops, SparseCore 0:
  9.2 42.3 all-gather.8
  57.1 55.4 all-gather.10
  154.2 100.0 all-reduce.4
  261.3 57.6 all-gather.10
  360.7 100.0 all-reduce.4
  472.2 64.3 reduce-scatter.1
